TPU v7x, 128 devices: a whole 4x4x4 slice. The times are simulated.
128 devices in a mesh: serve: 8 (over x, core), store: 16 (over z, y).
Axes of the slice: x: 4, y: 4, z: 4, core: 2. Of those that a mesh axis runs over, the one named last changes fastest.
Arguments:
- normalized_hidden_states: bfloat16 [65536, 2048], P(('serve', 'store')), may hold values from -20 to 20
- query_weight_matrix: bfloat16 [2048, 2048], replicated, may hold values from -0.125 to 0.125
- key_weight_matrix: bfloat16 [2048, 512], replicated, may hold values from -0.125 to 0.125
- value_weight_matrix: bfloat16 [2048, 512], replicated, may hold values from -0.125 to 0.125
- adapter_down_weight: bfloat16 [512, 32, 2048], P('store', None, 'serve'), may hold values from -0.125 to 0.125
- adapter_up_query_weight: bfloat16 [512, 16, 2048], P('store', None, 'serve'), may hold values from -1.5 to 1.5
- adapter_up_value_weight: bfloat16 [512, 16, 512], P('store', None, 'serve'), may hold values from -1.5 to 1.5
- adapter_panel_slot: int32 [512], replicated, may hold values from 0 to 511, as said below
- adapter_per_request: int32 [128, 16], P(('serve', 'store')), may hold values from 0 to 511, as said below
- request_token_length: int32 [128, 16], P(('serve', 'store')), may hold values from 1 to 64, 512 in all within a row
Outputs:
- attended: bfloat16 [65536, 2048], P(('serve', 'store'))
Inputs may be any that keep to these rules, and one draw needn't show every extreme that they name: Each number appears once; adapter a's panels are entry adapter_panel_slot[a] of the three panel arrays, whose owner is index adapter_panel_slot[a] // 32 of store. `adapter_per_request`: the 16 requests of one device use adapters of 16 different owners. `request_token_length`: each row sums to 512; the longest request of each device has exactly 64 tokens.
All inputs are finite; a program needn't handle non-finite values.
Results may differ from a plain program's by a relative error of at most 0.012.
Values may be sent and summed in bfloat16 or wider, within the bound.
No kernel may reach another device: no remote copies, remote signals or barrier semaphores. Data moves between devices by JAX's collectives and lax.ppermute only.
A program may use at most 128 MiB of HBM per device.

v0:
```python
import jax
import jax.numpy as jnp
from jax import lax
from jax.sharding import PartitionSpec as P

HEADS = 32
KV_HEADS = 8
HEAD_DIM = 64
ADAPTER_RANK = 16
ADP_DEV = 32
LEN_MAX = 64


def rotary(heads_in, positions):
    half_dim = HEAD_DIM // 2
    frequency = 500000.0 ** (-(jnp.arange(half_dim).astype(jnp.float32) * 2.0 / HEAD_DIM))
    angles = positions.astype(jnp.float32)[:, None] * frequency[None, :]
    cosine_table = jnp.cos(angles)[:, None, :]
    sine_table = jnp.sin(angles)[:, None, :]
    first_half = heads_in[..., :half_dim]
    second_half = heads_in[..., half_dim:]
    return jnp.concatenate(
        [
            first_half * cosine_table - second_half * sine_table,
            second_half * cosine_table + first_half * sine_table,
        ],
        axis=-1,
    )


def table_lookup(table, wanted):
    entries = jnp.arange(table.shape[0], dtype=jnp.int32)
    return jnp.sum(jnp.where(wanted[..., None] == entries, table, 0), axis=-1)


def reduced_rank_products(block_list, down_panels, up_query, up_value):
    low = jnp.einsum(
        "jkd,jrd->jkr", block_list, down_panels, preferred_element_type=jnp.float32
    ).astype(jnp.bfloat16)
    query_update = jnp.einsum(
        "jkr,jrd->jkd", low[..., :ADAPTER_RANK], up_query, preferred_element_type=jnp.float32
    ).astype(jnp.bfloat16)
    value_update = jnp.einsum(
        "jkr,jrd->jkd", low[..., ADAPTER_RANK:], up_value, preferred_element_type=jnp.float32
    ).astype(jnp.bfloat16)
    return (query_update, value_update)


def local_choice(panel_set, lists, adapter_panel_slot, my_store):
    source_slots = table_lookup(adapter_panel_slot, lists)
    mine_mask = source_slots // ADP_DEV == my_store
    local_source = jnp.sum(jnp.where(mine_mask, source_slots % ADP_DEV, 0), axis=1)
    return tuple((jnp.take(panel, local_source, axis=0) for panel in panel_set))


def attention(query_rot, key_rot, value_rows, request_ids):
    tok_rows = query_rot.shape[0]
    per_group = HEADS // KV_HEADS
    block_rows = min(128, tok_rows)
    reach = LEN_MAX
    key_pad = jnp.concatenate(
        [jnp.zeros((reach,) + key_rot.shape[1:], key_rot.dtype), key_rot], axis=0
    )
    value_pad = jnp.concatenate(
        [jnp.zeros((reach,) + value_rows.shape[1:], value_rows.dtype), value_rows], axis=0
    )
    ids_pad = jnp.concatenate([jnp.full((reach,), -1, jnp.int32), request_ids], axis=0)
    token_order = jnp.arange(tok_rows, dtype=jnp.int32)
    order_pad = jnp.concatenate([jnp.full((reach,), -1, jnp.int32), token_order], axis=0)
    outputs = []
    for block_index in range(tok_rows // block_rows):
        first = block_index * block_rows
        query_block = query_rot[first : first + block_rows]
        query_ids = request_ids[first : first + block_rows]
        query_order = token_order[first : first + block_rows]
        key_block = key_pad[first : first + reach + block_rows]
        value_block = value_pad[first : first + reach + block_rows]
        key_ids = ids_pad[first : first + reach + block_rows]
        key_order = order_pad[first : first + reach + block_rows]
        allowed = (query_ids[:, None] == key_ids[None, :]) & (
            key_order[None, :] <= query_order[:, None]
        )
        pieces = []
        for group_index in range(KV_HEADS):
            query_part = query_block[:, group_index * per_group : (group_index + 1) * per_group, :]
            key_part = key_block[:, group_index, :]
            value_part = value_block[:, group_index, :]
            scores = jnp.einsum(
                "qhd,kd->hqk", query_part, key_part, preferred_element_type=jnp.float32
            ) * HEAD_DIM ** (-0.5)
            scores = jnp.where(allowed[None], scores, -jnp.inf)
            row_max = jnp.max(scores, axis=-1, keepdims=True)
            raised = jnp.exp(scores - row_max)
            row_total = jnp.sum(raised, axis=-1)
            weights = raised.astype(jnp.bfloat16)
            mixed_heads = (
                jnp.einsum("hqk,kd->qhd", weights, value_part, preferred_element_type=jnp.float32)
                / jnp.transpose(row_total)[:, :, None]
            )
            pieces.append(mixed_heads)
        outputs.append(
            jnp.concatenate(pieces, axis=1)
            .reshape(block_rows, HEADS * HEAD_DIM)
            .astype(jnp.bfloat16)
        )
    return jnp.concatenate(outputs, axis=0)


def local(
    normalized_hidden_states,
    query_weight_matrix,
    key_weight_matrix,
    value_weight_matrix,
    adapter_down_weight,
    adapter_up_query_weight,
    adapter_up_value_weight,
    adapter_panel_slot,
    adapter_per_request,
    request_token_length,
):
    store_count = lax.axis_size("store")
    my_store = lax.axis_index("store")
    tok_rows = normalized_hidden_states.shape[0]
    request_count = request_token_length.shape[1]
    group_lists = lax.all_gather(adapter_per_request, "store", axis=0, tiled=True)
    lengths = request_token_length[0]
    adapters = adapter_per_request[0]
    request_ends = jnp.cumsum(lengths)
    starts = request_ends - lengths
    token_order = jnp.arange(tok_rows, dtype=jnp.int32)
    request_ids = jnp.sum((token_order[:, None] >= request_ends[None, :]).astype(jnp.int32), axis=1)
    member = request_ids[:, None] == jnp.arange(request_count, dtype=jnp.int32)[None, :]
    positions = token_order - jnp.sum(jnp.where(member, starts[None, :], 0), axis=1)
    slot_index_list = table_lookup(adapter_panel_slot, adapters)
    owners = slot_index_list // ADP_DEV
    owner_pick = owners[None, :] == jnp.arange(store_count, dtype=jnp.int32)[:, None]
    start_for = jnp.sum(jnp.where(owner_pick, starts[None, :], 0), axis=1)
    length_for = jnp.sum(jnp.where(owner_pick, lengths[None, :], 0), axis=1)
    offsets = jnp.arange(LEN_MAX, dtype=jnp.int32)
    valid_rows = offsets[None, :] < length_for[:, None]
    row_index = jnp.where(valid_rows, start_for[:, None] + offsets[None, :], 0)
    block_list = jnp.where(
        valid_rows[..., None], normalized_hidden_states[row_index], jnp.zeros((), jnp.bfloat16)
    )
    owner_token = jnp.sum(jnp.where(member, owners[None, :], 0), axis=1)
    back_index = owner_token * LEN_MAX + positions
    panels = (
        lax.all_gather(adapter_down_weight, "serve", axis=2, tiled=True),
        lax.all_gather(adapter_up_query_weight, "serve", axis=2, tiled=True),
        lax.all_gather(adapter_up_value_weight, "serve", axis=2, tiled=True),
    )
    down_chosen, upq_chosen, upv_chosen = local_choice(
        panels, group_lists, adapter_panel_slot, my_store
    )
    arrived = lax.all_to_all(block_list, "store", split_axis=0, concat_axis=0, tiled=True)
    query_update, value_update = reduced_rank_products(arrived, down_chosen, upq_chosen, upv_chosen)
    query_update, value_update = (
        lax.all_to_all(query_update, "store", split_axis=0, concat_axis=0, tiled=True),
        lax.all_to_all(value_update, "store", split_axis=0, concat_axis=0, tiled=True),
    )
    delta_query = query_update.reshape(-1, query_update.shape[2])[back_index]
    delta_value = value_update.reshape(-1, value_update.shape[2])[back_index]
    base_query = jnp.dot(
        normalized_hidden_states, query_weight_matrix, preferred_element_type=jnp.float32
    ) + delta_query.astype(jnp.float32)
    query_rot = rotary(base_query.reshape(tok_rows, HEADS, HEAD_DIM), positions).astype(
        jnp.bfloat16
    )
    base_key = jnp.dot(
        normalized_hidden_states, key_weight_matrix, preferred_element_type=jnp.float32
    )
    key_rot = rotary(base_key.reshape(tok_rows, KV_HEADS, HEAD_DIM), positions).astype(jnp.bfloat16)
    value_rows = (
        jnp.dot(normalized_hidden_states, value_weight_matrix, preferred_element_type=jnp.float32)
        + delta_value.astype(jnp.float32)
    ).astype(jnp.bfloat16)
    value_rows = value_rows.reshape(tok_rows, KV_HEADS, HEAD_DIM)
    return attention(query_rot, key_rot, value_rows, request_ids)


def solution(mesh):
    return jax.shard_map(
        local,
        mesh=mesh,
        in_specs=(
            P(("serve", "store"), None),
            P(),
            P(),
            P(),
            P("store", None, "serve"),
            P("store", None, "serve"),
            P("store", None, "serve"),
            P(),
            P(("serve", "store"), None),
            P(("serve", "store"), None),
        ),
        out_specs=P(("serve", "store"), None),
        check_vma=False,
    )
```

profile of v0, /device:TPU:6, one launch (start us, length us, event | category | flops | bytes accessed | tf_op | source)
XLA Modules:
  0.0 278.1 jit_solution(15129915523642141510)
XLA Ops:
  10.6 6.1 %gather_fusion = bf16[1024,2048]{1,0:T(8,128)(2,1)} fusion(bf16[512,2048]{1,0:T(8,128)(2,1)S(1)} %copy-done, s32[1024]{0:T(1024)S(1)} %broadcast_clamp_fusion), kind=kCustom, calls=%fused_computation | custom fusion | bytes 8392704 | tf_op jit(solution)/shard_map/gather | solution.py:143
  16.8 4.5 %broadcast_select_fusion = bf16[16,64,2048]{2,1,0:T(8,128)(2,1)} fusion(bf16[16,64,2048]{2,1,0:T(8,128)(2,1)} %bitcast.784, pred[16,64]{1,0:T(8,128)(4,1)S(1)} %iota_compare_fusion.6), kind=kLoop, calls=%fused_computation.69 | loop fusion | flops 2097152 | bytes 8389632 | tf_op jit(solution)/shard_map/jit(_where)/select_n | solution.py:142
  21.3 8.3 %all-to-all-start = ((bf16[16,64,2048]{2,1,0:T(8,128)(2,1)}), bf16[16,64,2048]{2,1,0:T(8,128)(2,1)}, u32[]{:S(2)}, u32[]{:S(2)}) async-start(bf16[16,64,2048]{2,1,0:T(8,128)(2,1)} %broadcast_select_fusion), calls=%async_computation | async-start | bytes 8388608 | tf_op jit(solution)/shard_map/all_to_all | solution.py:155
  30.6 21.4 %all_gather.14 = bf16[32,16,512]{0,1,2:T(8,128)(2,1)} all-gather(bf16[32,16,64]{0,1,2:T(8,128)(2,1)S(1)} %copy.78), channel_id=1, replica_groups=mesh['serve'=8,'store'=16] {'serve'}, dimensions={2}, use_global_device_ids=true | all-gather | bytes 589824 | tf_op jit(solution)/shard_map/all_gather | solution.py:150
  52.1 3.1 %copy.79 = bf16[32,16,512]{2,1,0:T(8,128)(2,1)S(1)} copy(bf16[32,16,512]{0,1,2:T(8,128)(2,1)} %all_gather.14) | data formatting | bytes 1048576 | tf_op jit(solution)/shard_map/all_gather | solution.py:150
  55.2 48.8 %all-gather = s32[16,1,16]{2,1,0:T(1,128)S(1)} all-gather(s32[1,1,16]{2,1,0:T(1,128)S(1)} %bitcast.854), channel_id=1, replica_groups=mesh['serve'=8,'store'=16] {'store'}, dimensions={0}, use_global_device_ids=true | all-gather | bytes 1088 | tf_op jit(solution)/shard_map/all_gather | solution.py:125
  105.2 4.2 %gather_fusion.1 = bf16[16,32,2048]{2,1,0:T(8,128)(2,1)} fusion(bf16[32,32,2048]{2,1,0:T(8,128)(2,1)} %all-gather.4.cloned.1.call-done, s32[1024]{0:T(1024)S(1)} %pad_clamp_fusion.1), kind=kCustom, calls=%fused_computation.1 | custom fusion | bytes 4194368 | tf_op jit(solution)/shard_map/jit(_take)/gather | solution.py:53
  109.4 4.1 %fusion.68 = bf16[16,64,32]{1,2,0:T(8,128)(2,1)S(1)} fusion(bf16[16,64,2048]{2,1,0:T(8,128)(2,1)} %all-to-all-done, bf16[16,32,2048]{2,1,0:T(8,128)(2,1)} %gather_fusion.1, pred[16]{0:T(512)(128)(4,1)S(1)} %compare_and_fusion.4), kind=kOutput, calls=%fused_computation.225 | convolution fusion | flops 135299072 | bytes 6357008 | tf_op jit(solution)/shard_map/jkd,jrd->jkr/dot_general | solution.py:37
  115.0 4.6 %all-to-all-start.1 = ((bf16[16,64,512]{2,1,0:T(8,128)(2,1)}), bf16[16,64,512]{2,1,0:T(8,128)(2,1)}, u32[]{:S(2)}, u32[]{:S(2)}) async-start(bf16[16,64,512]{2,1,0:T(8,128)(2,1)} %convolution_convert_fusion.1), calls=%async_computation.1 | async-start | bytes 2097152 | tf_op jit(solution)/shard_map/all_to_all | solution.py:159
  119.7 3.2 %gather_fusion.4 = bf16[16,16,2048]{2,1,0:T(8,128)(2,1)} fusion(bf16[32,16,2048]{2,1,0:T(8,128)(2,1)} %all-gather.6.cloned.1.call-done, s32[1024]{0:T(1024)S(1)} %pad_clamp_fusion.1), kind=kCustom, calls=%fused_computation.4 | custom fusion | bytes 2097216 | tf_op jit(solution)/shard_map/jit(_take)/gather | solution.py:53
  122.8 4.5 %convolution_convert_fusion = bf16[16,64,2048]{2,1,0:T(8,128)(2,1)} fusion(bf16[16,16,2048]{2,1,0:T(8,128)(2,1)} %gather_fusion.4, pred[16]{0:T(512)(128)(4,1)S(1)} %compare_and_fusion.4, bf16[16,64,32]{1,2,0:T(8,128)(2,1)S(1)} %fusion.68), kind=kOutput, calls=%fused_computation.70 | convolution fusion | flops 69730304 | bytes 5308928 | tf_op jit(solution)/shard_map/jkr,jrd->jkd/dot_general | solution.py:40
  127.3 6.5 %all-to-all-done.1 = bf16[16,64,512]{2,1,0:T(8,128)(2,1)} async-done(((bf16[16,64,512]{2,1,0:T(8,128)(2,1)}), bf16[16,64,512]{2,1,0:T(8,128)(2,1)}, u32[]{:S(2)}, u32[]{:S(2)}) %all-to-all-start.1) | async-done | bytes 1048608 | tf_op jit(solution)/shard_map/all_to_all | solution.py:159
  133.8 4.7 %all-to-all-start.2 = ((bf16[16,64,2048]{2,1,0:T(8,128)(2,1)}), bf16[16,64,2048]{2,1,0:T(8,128)(2,1)}, u32[]{:S(2)}, u32[]{:S(2)}) async-start(bf16[16,64,2048]{2,1,0:T(8,128)(2,1)} %convolution_convert_fusion), calls=%async_computation.2 | async-start | bytes 8388608 | tf_op jit(solution)/shard_map/all_to_all | solution.py:158
  139.3 2.9 %fusion.563 = f32[512,512]{0,1:T(8,128)S(1)} fusion(bf16[512,2048]{1,0:T(8,128)(2,1)S(1)} %copy-done, bf16[2048,512]{1,0:T(8,128)(2,1)} %param.12), kind=kOutput, calls=%fused_computation.765 | convolution fusion | flops 1073741824 | bytes 5242880 | tf_op jit(solution)/shard_map/dot_general | solution.py:169
  143.7 3.3 %gather_fusion.3 = bf16[512,512]{1,0:T(8,128)(2,1)S(1)} fusion(bf16[1024,512]{1,0:T(8,128)(2,1)} %bitcast.9, s32[1024]{0:T(1024)S(1)} %pad_clamp_fusion), kind=kCustom, calls=%fused_computation.3 | custom fusion | bytes 1050624 | tf_op jit(solution)/shard_map/gather | solution.py:162
  147.1 3.6 %fusion.3 = bf16[512,512]{1,0:T(8,128)(2,1)} fusion(bf16[512,2048]{1,0:T(8,128)(2,1)S(1)} %copy-done, bf16[2048,512]{1,0:T(8,128)(2,1)} %param.13, bf16[512,512]{1,0:T(8,128)(2,1)S(1)} %gather_fusion.3), kind=kOutput, calls=%fused_computation.128 | convolution fusion | flops 1074528256 | bytes 5242880 | tf_op jit(solution)/shard_map/dot_general | solution.py:174
  159.2 30.4 %all-to-all-done.2 = bf16[16,64,2048]{2,1,0:T(8,128)(2,1)} async-done(((bf16[16,64,2048]{2,1,0:T(8,128)(2,1)}), bf16[16,64,2048]{2,1,0:T(8,128)(2,1)}, u32[]{:S(2)}, u32[]{:S(2)}) %all-to-all-start.2) | async-done | bytes 4194336 | tf_op jit(solution)/shard_map/all_to_all | solution.py:158
  189.6 8.0 %gather_fusion.5 = bf16[512,2048]{1,0:T(8,128)(2,1)} fusion(bf16[1024,2048]{1,0:T(8,128)(2,1)} %bitcast.19, s32[1024]{0:T(1024)S(1)} %pad_clamp_fusion), kind=kCustom, calls=%fused_computation.5 | custom fusion | bytes 4196352 | tf_op jit(solution)/shard_map/gather | solution.py:161
  197.5 9.7 %convert_add_fusion = f32[512,2048]{1,0:T(8,128)} fusion(bf16[512,2048]{1,0:T(8,128)(2,1)} %gather_fusion.5, bf16[512,2048]{1,0:T(8,128)(2,1)S(1)} %copy-done, bf16[2048,2048]{1,0:T(8,128)(2,1)} %param.11), kind=kOutput, calls=%fused_computation.68 | convolution fusion | flops 4297064448 | bytes 16777216 | tf_op jit(solution)/shard_map/dot_general | solution.py:163
  207.3 5.3 %copy.81 = f32[512,2048]{0,1:T(8,128)} copy(f32[512,2048]{1,0:T(8,128)} %convert_add_fusion) | data formatting | bytes 8388608 | tf_op jit(solution)/shard_map/add | solution.py:163
  212.6 2.9 %add_convert_fusion = (bf16[512,32,32]{0,2,1:T(8,128)(2,1)S(1)}, bf16[512,32,32]{0,2,1:T(8,128)(2,1)S(1)}) fusion(f32[512,32,64]{0,2,1:T(8,128)} %bitcast.785, f32[512,32]{0,1:T(8,128)S(1)} %get-tuple-element.17, f32[512,32]{0,1:T(8,128)S(1)} %get-tuple-element.16), kind=kLoop, calls=%fused_computation.121 | loop fusion | flops 4194304 | bytes 6422528 | tf_op jit(solution)/shard_map/convert.33
  253.7 2.1 copy.87
  261.5 2.1 copy.86
  268.4 2.9 %pad_maximum_fusion.1 = bf16[512,2048]{1,0:T(8,128)(2,1)} fusion(bf16[128,2048]{1,0:T(8,128)(2,1)} %copy.88, bf16[128,2048]{1,0:T(8,128)(2,1)} %copy.87, bf16[128,2048]{1,0:T(8,128)(2,1)} %copy.86, bf16[128,2048]{1,0:T(8,128)(2,1)S(1)} %copy.85), kind=kLoop, calls=%fused_computation.120 | loop fusion | flops 8388608 | bytes 4194304 | tf_op jit(solution)/shard_map/concatenate | solution.py:106
  (228 shorter events, 66.5 us)
Async XLA Ops:
  6.5 4.1 %copy-start = (bf16[512,2048]{1,0:T(8,128)(2,1)S(1)}, bf16[512,2048]{1,0:T(8,128)(2,1)}, u32[]{:S(2)}) copy-start(bf16[512,2048]{1,0:T(8,128)(2,1)} %param.10) | copy-start | bytes 6291460
  6.5 98.7 %all-gather.4.cloned.1.call-start = ((), (), s32[]{:S(2)}) async-start(), calls=%async_computation.3 | async-start | bytes 4718592 | tf_op jit(solution)/shard_map/all_gather | solution.py:148
  21.3 9.0 %copy-start.32 = (bf16[32,16,64]{2,1,0:T(8,128)(2,1)S(1)}, bf16[32,16,64]{2,1,0:T(8,128)(2,1)}, u32[]{:S(2)}) copy-start(bf16[32,16,64]{2,1,0:T(8,128)(2,1)} %param.16) | copy-start | bytes 196612
  21.3 88.1 %all-to-all-start = ((bf16[16,64,2048]{2,1,0:T(8,128)(2,1)}), bf16[16,64,2048]{2,1,0:T(8,128)(2,1)}, u32[]{:S(2)}, u32[]{:S(2)}) async-start(bf16[16,64,2048]{2,1,0:T(8,128)(2,1)} %broadcast_select_fusion), calls=%async_computation | async-start | bytes 8388608 | tf_op jit(solution)/shard_map/all_to_all | solution.py:155
  29.6 90.1 %all-gather.6.cloned.1.call-start = ((), (), s32[]{:S(2)}) async-start(), calls=%async_computation.4 | async-start | bytes 2359296 | tf_op jit(solution)/shard_map/all_gather | solution.py:149
  30.6 24.6 %copy-start.35 = (s32[1,16]{1,0:T(1,128)S(1)}, s32[1,16]{1,0:T(1,128)}, u32[]{:S(2)}) copy-start(s32[1,16]{1,0:T(1,128)} %param.18) | copy-start | bytes 196
  30.6 73.4 %copy-start.33 = (s32[512]{0:T(512)S(1)}, s32[512]{0:T(512)}, u32[]{:S(2)}) copy-start(s32[512]{0:T(512)} %param.17) | copy-start | bytes 6148
  115.0 18.8 %all-to-all-start.1 = ((bf16[16,64,512]{2,1,0:T(8,128)(2,1)}), bf16[16,64,512]{2,1,0:T(8,128)(2,1)}, u32[]{:S(2)}, u32[]{:S(2)}) async-start(bf16[16,64,512]{2,1,0:T(8,128)(2,1)} %convolution_convert_fusion.1), calls=%async_computation.1 | async-start | bytes 2097152 | tf_op jit(solution)/shard_map/all_to_all | solution.py:159
  133.8 55.8 %all-to-all-start.2 = ((bf16[16,64,2048]{2,1,0:T(8,128)(2,1)}), bf16[16,64,2048]{2,1,0:T(8,128)(2,1)}, u32[]{:S(2)}, u32[]{:S(2)}) async-start(bf16[16,64,2048]{2,1,0:T(8,128)(2,1)} %convolution_convert_fusion), calls=%async_computation.2 | async-start | bytes 8388608 | tf_op jit(solution)/shard_map/all_to_all | solution.py:158
  138.8 3.4 %copy-start.34 = (s32[512]{0:T(512)}, s32[512]{0:T(512)S(1)}, u32[]{:S(2)}) copy-start(s32[512]{0:T(512)S(1)} %iota.56) | copy-start | bytes 6148
  244.2 3.7 %copy-start.24 = (f32[4,128,192]{1,2,0:T(8,128)S(1)}, f32[4,128,192]{1,2,0:T(8,128)}, u32[]{:S(2)}) copy-start(f32[4,128,192]{1,2,0:T(8,128)} %get-tuple-element.43) | copy-start | bytes 1179652
  244.5 4.5 %copy-start.23 = (f32[4,128,192]{1,2,0:T(8,128)S(1)}, f32[4,128,192]{1,2,0:T(8,128)}, u32[]{:S(2)}) copy-start(f32[4,128,192]{1,2,0:T(8,128)} %get-tuple-element.45) | copy-start | bytes 1179652
  244.9 5.3 %copy-start.22 = (f32[4,128,192]{1,2,0:T(8,128)S(1)}, f32[4,128,192]{1,2,0:T(8,128)}, u32[]{:S(2)}) copy-start(f32[4,128,192]{1,2,0:T(8,128)} %get-tuple-element.47) | copy-start | bytes 1179652
  245.9 5.4 %copy-start.21 = (f32[4,128,192]{1,2,0:T(8,128)S(1)}, f32[4,128,192]{1,2,0:T(8,128)}, u32[]{:S(2)}) copy-start(f32[4,128,192]{1,2,0:T(8,128)} %get-tuple-element.49) | copy-start | bytes 1179652
  248.0 3.4 %copy-start.30 = (bf16[192,512]{0,1:T(8,128)(2,1)S(1)}, bf16[192,512]{0,1:T(8,128)(2,1)}, u32[]{:S(2)}) copy-start(bf16[192,512]{0,1:T(8,128)(2,1)} %copy.83) | copy-start | bytes 589828
  248.0 3.6 %copy-start.20 = (f32[4,128,192]{1,2,0:T(8,128)S(1)}, f32[4,128,192]{1,2,0:T(8,128)}, u32[]{:S(2)}) copy-start(f32[4,128,192]{1,2,0:T(8,128)} %get-tuple-element.51) | copy-start | bytes 1179652
  252.0 3.8 %copy-start.16 = (f32[4,128,192]{1,2,0:T(8,128)S(1)}, f32[4,128,192]{1,2,0:T(8,128)}, u32[]{:S(2)}) copy-start(f32[4,128,192]{1,2,0:T(8,128)} %get-tuple-element.59) | copy-start | bytes 1179652
  252.3 4.5 %copy-start.15 = (f32[4,128,192]{1,2,0:T(8,128)S(1)}, f32[4,128,192]{1,2,0:T(8,128)}, u32[]{:S(2)}) copy-start(f32[4,128,192]{1,2,0:T(8,128)} %get-tuple-element.61) | copy-start | bytes 1179652
  252.6 5.3 %copy-start.14 = (f32[4,128,192]{1,2,0:T(8,128)S(1)}, f32[4,128,192]{1,2,0:T(8,128)}, u32[]{:S(2)}) copy-start(f32[4,128,192]{1,2,0:T(8,128)} %get-tuple-element.63) | copy-start | bytes 1179652
  253.7 5.4 %copy-start.13 = (f32[4,128,192]{1,2,0:T(8,128)S(1)}, f32[4,128,192]{1,2,0:T(8,128)}, u32[]{:S(2)}) copy-start(f32[4,128,192]{1,2,0:T(8,128)} %get-tuple-element.65) | copy-start | bytes 1179652
  255.9 3.6 %copy-start.12 = (f32[4,128,192]{1,2,0:T(8,128)S(1)}, f32[4,128,192]{1,2,0:T(8,128)}, u32[]{:S(2)}) copy-start(f32[4,128,192]{1,2,0:T(8,128)} %get-tuple-element.67) | copy-start | bytes 1179652
  259.8 3.8 %copy-start.8 = (f32[4,128,192]{1,2,0:T(8,128)S(1)}, f32[4,128,192]{1,2,0:T(8,128)}, u32[]{:S(2)}) copy-start(f32[4,128,192]{1,2,0:T(8,128)} %get-tuple-element.75) | copy-start | bytes 1179652
  260.1 3.7 %copy-start.7 = (f32[4,128,192]{1,2,0:T(8,128)S(1)}, f32[4,128,192]{1,2,0:T(8,128)}, u32[]{:S(2)}) copy-start(f32[4,128,192]{1,2,0:T(8,128)} %get-tuple-element.77) | copy-start | bytes 1179652
  267.0 4.3 %copy-start.1 = (bf16[512,2048]{1,0:T(8,128)(2,1)S(1)}, bf16[512,2048]{1,0:T(8,128)(2,1)}, u32[]{:S(2)}) copy-start(bf16[512,2048]{1,0:T(8,128)(2,1)} %param.10) | copy-start | bytes 6291460
  (19 other events, 28.9 us)
Sparse Core Ops, SparseCore 0:
  9.0 44.3 all-gather.3
  55.1 27.0 all-gather.5
where the time goes:
time: 279 us; the launch traced here: 278 us
  blocking collectives  70.2 us (25%)
  matrix products  64.4 us (23%)
  local copies, waits for them, and re-layouts  55.3 us (20%)
  waiting for transfers between devices  38.3 us (14%)
  other arithmetic  17.9 us (6%)
  starting transfers between devices  17.6 us (6%)
  between operations  14.4 us (5%)
    all_gather x1, blocking collectives, local(): lax.all_gather(adapter_per_request, 'store', axis=0, tiled=True)  48.8 us
    all_to_all x1, waiting for transfers between devices, local(): lax.all_to_all(query_update, 'store', split_axis=0, concat_axis=0, tiled=...  30.4 us
    dot_general x32, matrix products, attention(): jnp.einsum('qhd,kd->hqk', query_part, key_part, preferred_element_type=jn...  26.6 us
    all_gather x1, blocking collectives, local(): lax.all_gather(adapter_up_value_weight, 'serve', axis=2, tiled=True)  21.4 us
    dot_general x32, matrix products, attention(): jnp.einsum('hqk,kd->qhd', weights, value_part, preferred_element_type=jnp...  11.5 us
    dot_general x1, matrix products, local(): jnp.dot(normalized_hidden_states, query_weight_matrix, preferred_element_...  9.7 us
    all_to_all x1, starting transfers between devices, local(): lax.all_to_all(block_list, 'store', split_axis=0, concat_axis=0, tiled=True)  8.28 us
    gather x1, local copies, waits for them, and re-layouts, local(): delta_query = query_update.reshape(-1, query_update.shape[2])[back_index]  7.95 us
  transfers between devices with their start and end apart: 5, of which 2 were waited for; matrix products, arithmetic and copies ran while one was open for 20% of the time, Pallas kernels for 0%

commit v1 on v0

--- a/solution.py
+++ b/solution.py
@@ -9,6 +9,19 @@
 ADAPTER_RANK = 16
 ADP_DEV = 32
 LEN_MAX = 64
+
+
+def collect(value, axis, dim):
+    ways = lax.axis_size(axis)
+    up = [(d, (d + 1) % ways) for d in range(ways)]
+    down = [(d, (d - 1) % ways) for d in range(ways)]
+    earlier, later = ([value], [value])
+    for _ in range(ways // 2):
+        earlier.append(lax.ppermute(earlier[-1], axis, up))
+    for _ in range((ways - 1) // 2):
+        later.append(lax.ppermute(later[-1], axis, down))
+    line = jnp.concatenate([*earlier[::-1], *later[1:]], axis=dim)
+    return jnp.roll(line, (lax.axis_index(axis) - ways // 2) * value.shape[dim], axis=dim)
 
 
 def rotary(heads_in, positions):
@@ -147,7 +160,7 @@
     panels = (
         lax.all_gather(adapter_down_weight, "serve", axis=2, tiled=True),
         lax.all_gather(adapter_up_query_weight, "serve", axis=2, tiled=True),
-        lax.all_gather(adapter_up_value_weight, "serve", axis=2, tiled=True),
+        collect(adapter_up_value_weight, "serve", 2),
     )
     down_chosen, upq_chosen, upv_chosen = local_choice(
         panels, group_lists, adapter_panel_slot, my_store

time: 279 us -> 313 us (1.12)
  waiting for transfers between devices: 38.3 us -> 61 us
  starting transfers between devices: 17.6 us -> 22.8 us
  local copies, waits for them, and re-layouts: 55.3 us -> 59 us
    all_gather x1, blocking collectives: 48.8 us -> 71.9 us  [local(): lax.all_gather(adapter_per_request, 'store', axis=0, tiled=True)]
    all_gather x1 -> x0, blocking collectives: 21.4 us -> none  [local(): lax.all_gather(adapter_up_value_weight, 'serve', axis=2, tiled=True)]
    all_to_all x1, waiting for transfers between devices: 30.4 us -> 40.2 us  [local(): lax.all_to_all(query_update, 'store', split_axis=0, concat_axis=0, tiled=...]
    ppermute x0 -> x7, waiting for transfers between devices: none -> 8.45 us  [the longest x4 8.45 us: collect(): earlier.append(lax.ppermute(earlier[-1], axis, up))]
    ppermute x0 -> x7, starting transfers between devices: none -> 5.21 us  [the longest x3 5.17 us: collect(): later.append(lax.ppermute(later[-1], axis, down))]
    all_to_all x1, waiting for transfers between devices: 6.49 us -> 10.8 us  [local(): lax.all_to_all(value_update, 'store', split_axis=0, concat_axis=0, tiled=...]
  transfers between devices with their start and end apart: 5 -> 12, of which waited for: 2 -> 5; matrix products, arithmetic and copies ran while one was open for 20% -> 19% of each run, Pallas kernels for 0% -> 0%
where the time goes in v1:
time: 313 us; the launch traced here: 311 us
  blocking collectives  71.9 us (23%)
  matrix products  64.3 us (21%)
  waiting for transfers between devices  61 us (19%)
  local copies, waits for them, and re-layouts  59 us (19%)
  starting transfers between devices  22.8 us (7%)
  other arithmetic  17.9 us (6%)
  between operations  14.4 us (5%)
    all_gather x1, blocking collectives, local(): lax.all_gather(adapter_per_request, 'store', axis=0, tiled=True)  71.9 us
    all_to_all x1, waiting for transfers between devices, local(): lax.all_to_all(query_update, 'store', split_axis=0, concat_axis=0, tiled=...  40.2 us
    dot_general x32, matrix products, attention(): jnp.einsum('qhd,kd->hqk', query_part, key_part, preferred_element_type=jn...  26.6 us
    dot_general x32, matrix products, attention(): jnp.einsum('hqk,kd->qhd', weights, value_part, preferred_element_type=jnp...  11.5 us
    all_to_all x1, waiting for transfers between devices, local(): lax.all_to_all(value_update, 'store', split_axis=0, concat_axis=0, tiled=...  10.8 us
    dot_general x1, matrix products, local(): jnp.dot(normalized_hidden_states, query_weight_matrix, preferred_element_...  9.7 us
    gather x3, local copies, waits for them, and re-layouts, local_choice(): return tuple((jnp.take(panel, local_source, axis=0) for panel in panel_set))  8.96 us
    ppermute x4, waiting for transfers between devices, collect(): earlier.append(lax.ppermute(earlier[-1], axis, up))  8.45 us
  transfers between devices with their start and end apart: 12, of which 5 were waited for; matrix products, arithmetic and copies ran while one was open for 19% of the time, Pallas kernels for 0%

profile of v1, /device:TPU:6, one launch (start us, length us, event | category | flops | bytes accessed | tf_op | source)
XLA Modules:
  0.0 311.3 jit_solution(16584328445695789760)
XLA Ops:
  10.6 6.1 %gather_fusion = bf16[1024,2048]{1,0:T(8,128)(2,1)} fusion(bf16[512,2048]{1,0:T(8,128)(2,1)S(1)} %copy-done, s32[1024]{0:T(1024)S(1)} %broadcast_clamp_fusion), kind=kCustom, calls=%fused_computation | custom fusion | bytes 8392704 | tf_op jit(solution)/shard_map/gather | solution.py:156
  16.8 4.5 %broadcast_select_fusion = bf16[16,64,2048]{2,1,0:T(8,128)(2,1)} fusion(bf16[16,64,2048]{2,1,0:T(8,128)(2,1)} %bitcast.785, pred[16,64]{1,0:T(8,128)(4,1)S(1)} %iota_compare_fusion.6), kind=kLoop, calls=%fused_computation.69 | loop fusion | flops 2097152 | bytes 8389632 | tf_op jit(solution)/shard_map/jit(_where)/select_n | solution.py:155
  21.3 8.3 %all-to-all-start = ((bf16[16,64,2048]{2,1,0:T(8,128)(2,1)}), bf16[16,64,2048]{2,1,0:T(8,128)(2,1)}, u32[]{:S(2)}, u32[]{:S(2)}) async-start(bf16[16,64,2048]{2,1,0:T(8,128)(2,1)} %broadcast_select_fusion), calls=%async_computation | async-start | bytes 8388608 | tf_op jit(solution)/shard_map/all_to_all | solution.py:168
  32.1 71.9 %all-gather = s32[16,1,16]{2,1,0:T(1,128)S(1)} all-gather(s32[1,1,16]{2,1,0:T(1,128)S(1)} %bitcast.855), channel_id=1, replica_groups=mesh['serve'=8,'store'=16] {'store'}, dimensions={0}, use_global_device_ids=true | all-gather | bytes 1088 | tf_op jit(solution)/shard_map/all_gather | solution.py:138
  106.4 2.6 collective-permute-done.1
  110.8 2.6 collective-permute-done.2
  114.7 3.2 %collective-permute-done.3 = bf16[32,16,64]{2,1,0:T(8,128)(2,1)} collective-permute-done((bf16[32,16,64]{2,1,0:T(8,128)(2,1)S(1)}, bf16[32,16,64]{2,1,0:T(8,128)(2,1)}, u32[]{:S(2)}, u32[]{:S(2)}) %collective-permute-start.3) | collective-permute-done | bytes 65568 | tf_op jit(solution)/shard_map/ppermute | solution.py:20
  117.9 2.6 concatenate.43
  123.3 4.2 %gather_fusion.1 = bf16[16,32,2048]{2,1,0:T(8,128)(2,1)} fusion(bf16[32,32,2048]{2,1,0:T(8,128)(2,1)} %all-gather.4.cloned.1.call-done, s32[1024]{0:T(1024)S(1)} %pad_clamp_fusion.1), kind=kCustom, calls=%fused_computation.1 | custom fusion | bytes 4194368 | tf_op jit(solution)/shard_map/jit(_take)/gather | solution.py:66
  127.5 4.1 %fusion.68 = bf16[16,64,32]{1,2,0:T(8,128)(2,1)S(1)} fusion(bf16[16,64,2048]{2,1,0:T(8,128)(2,1)} %all-to-all-done, bf16[16,32,2048]{2,1,0:T(8,128)(2,1)} %gather_fusion.1, pred[16]{0:T(512)(128)(4,1)S(1)} %compare_and_fusion.4), kind=kOutput, calls=%fused_computation.225 | convolution fusion | flops 135299072 | bytes 6357008 | tf_op jit(solution)/shard_map/jkd,jrd->jkr/dot_general | solution.py:50
  133.1 4.5 %all-to-all-start.1 = ((bf16[16,64,512]{2,1,0:T(8,128)(2,1)}), bf16[16,64,512]{2,1,0:T(8,128)(2,1)S(1)}, u32[]{:S(2)}, u32[]{:S(2)}) async-start(bf16[16,64,512]{2,1,0:T(8,128)(2,1)} %convolution_convert_fusion.1), calls=%async_computation.1 | async-start | bytes 2097152 | tf_op jit(solution)/shard_map/all_to_all | solution.py:172
  137.7 3.2 %gather_fusion.4 = bf16[16,16,2048]{2,1,0:T(8,128)(2,1)} fusion(bf16[32,16,2048]{2,1,0:T(8,128)(2,1)} %all-gather.6.cloned.1.call-done, s32[1024]{0:T(1024)S(1)} %pad_clamp_fusion.1), kind=kCustom, calls=%fused_computation.4 | custom fusion | bytes 2097216 | tf_op jit(solution)/shard_map/jit(_take)/gather | solution.py:66
  140.9 4.5 %convolution_convert_fusion = bf16[16,64,2048]{2,1,0:T(8,128)(2,1)} fusion(bf16[16,16,2048]{2,1,0:T(8,128)(2,1)} %gather_fusion.4, pred[16]{0:T(512)(128)(4,1)S(1)} %compare_and_fusion.4, bf16[16,64,32]{1,2,0:T(8,128)(2,1)S(1)} %fusion.68), kind=kOutput, calls=%fused_computation.70 | convolution fusion | flops 69730304 | bytes 5308928 | tf_op jit(solution)/shard_map/jkr,jrd->jkd/dot_general | solution.py:53
  145.3 10.8 %all-to-all-done.1 = bf16[16,64,512]{2,1,0:T(8,128)(2,1)S(1)} async-done(((bf16[16,64,512]{2,1,0:T(8,128)(2,1)}), bf16[16,64,512]{2,1,0:T(8,128)(2,1)S(1)}, u32[]{:S(2)}, u32[]{:S(2)}) %all-to-all-start.1) | async-done | bytes 1048608 | tf_op jit(solution)/shard_map/all_to_all | solution.py:172
  157.1 4.7 %all-to-all-start.2 = ((bf16[16,64,2048]{2,1,0:T(8,128)(2,1)}), bf16[16,64,2048]{2,1,0:T(8,128)(2,1)}, u32[]{:S(2)}, u32[]{:S(2)}) async-start(bf16[16,64,2048]{2,1,0:T(8,128)(2,1)} %convolution_convert_fusion), calls=%async_computation.2 | async-start | bytes 8388608 | tf_op jit(solution)/shard_map/all_to_all | solution.py:171
  162.6 2.9 fusion.563
  167.1 3.3 %gather_fusion.3 = bf16[512,512]{1,0:T(8,128)(2,1)S(1)} fusion(bf16[1024,512]{1,0:T(8,128)(2,1)} %bitcast.784, s32[1024]{0:T(1024)S(1)} %pad_clamp_fusion), kind=kCustom, calls=%fused_computation.3 | custom fusion | bytes 1050624 | tf_op jit(solution)/shard_map/gather | solution.py:175
  170.4 3.6 %fusion.3 = bf16[512,512]{1,0:T(8,128)(2,1)} fusion(bf16[512,2048]{1,0:T(8,128)(2,1)S(1)} %copy-done, bf16[2048,512]{1,0:T(8,128)(2,1)} %param.13, bf16[512,512]{1,0:T(8,128)(2,1)S(1)} %gather_fusion.3), kind=kOutput, calls=%fused_computation.128 | convolution fusion | flops 1074528256 | bytes 5242880 | tf_op jit(solution)/shard_map/dot_general | solution.py:187
  182.6 40.2 %all-to-all-done.2 = bf16[16,64,2048]{2,1,0:T(8,128)(2,1)} async-done(((bf16[16,64,2048]{2,1,0:T(8,128)(2,1)}), bf16[16,64,2048]{2,1,0:T(8,128)(2,1)}, u32[]{:S(2)}, u32[]{:S(2)}) %all-to-all-start.2) | async-done | bytes 4194336 | tf_op jit(solution)/shard_map/all_to_all | solution.py:171
  222.9 8.0 %gather_fusion.5 = bf16[512,2048]{1,0:T(8,128)(2,1)} fusion(bf16[1024,2048]{1,0:T(8,128)(2,1)} %bitcast.19, s32[1024]{0:T(1024)S(1)} %pad_clamp_fusion), kind=kCustom, calls=%fused_computation.5 | custom fusion | bytes 4196352 | tf_op jit(solution)/shard_map/gather | solution.py:174
  230.8 9.7 %convert_add_fusion = f32[512,2048]{1,0:T(8,128)} fusion(bf16[512,2048]{1,0:T(8,128)(2,1)} %gather_fusion.5, bf16[512,2048]{1,0:T(8,128)(2,1)S(1)} %copy-done, bf16[2048,2048]{1,0:T(8,128)(2,1)} %param.11), kind=kOutput, calls=%fused_computation.68 | convolution fusion | flops 4297064448 | bytes 16777216 | tf_op jit(solution)/shard_map/dot_general | solution.py:176
  240.5 5.3 %copy.65 = f32[512,2048]{0,1:T(8,128)} copy(f32[512,2048]{1,0:T(8,128)} %convert_add_fusion) | data formatting | bytes 8388608 | tf_op jit(solution)/shard_map/add | solution.py:176
  245.9 2.9 add_convert_fusion
  301.6 2.9 pad_maximum_fusion.1
  (255 shorter events, 80.1 us)
Async XLA Ops:
  6.5 116.7 %all-gather.4.cloned.1.call-start = ((), (), s32[]{:S(2)}) async-start(), calls=%async_computation.3 | async-start | bytes 4718592 | tf_op jit(solution)/shard_map/all_gather | solution.py:161
  21.3 9.0 %copy-start.27 = (bf16[32,16,64]{2,1,0:T(8,128)(2,1)S(1)}, bf16[32,16,64]{2,1,0:T(8,128)(2,1)}, u32[]{:S(2)}) copy-start(bf16[32,16,64]{2,1,0:T(8,128)(2,1)} %param.16) | copy-start | bytes 196612
  21.3 10.8 %copy-start.42 = (s32[1,16]{1,0:T(1,128)S(1)}, s32[1,16]{1,0:T(1,128)}, u32[]{:S(2)}) copy-start(s32[1,16]{1,0:T(1,128)} %param.18) | copy-start | bytes 196
  21.3 82.7 %copy-start.38 = (s32[512]{0:T(512)S(1)}, s32[512]{0:T(512)}, u32[]{:S(2)}) copy-start(s32[512]{0:T(512)} %param.17) | copy-start | bytes 6148
  21.3 106.2 %all-to-all-start = ((bf16[16,64,2048]{2,1,0:T(8,128)(2,1)}), bf16[16,64,2048]{2,1,0:T(8,128)(2,1)}, u32[]{:S(2)}, u32[]{:S(2)}) async-start(bf16[16,64,2048]{2,1,0:T(8,128)(2,1)} %broadcast_select_fusion), calls=%async_computation | async-start | bytes 8388608 | tf_op jit(solution)/shard_map/all_to_all | solution.py:168
  29.6 108.1 %all-gather.6.cloned.1.call-start = ((), (), s32[]{:S(2)}) async-start(), calls=%async_computation.4 | async-start | bytes 2359296 | tf_op jit(solution)/shard_map/all_gather | solution.py:162
  30.3 74.3 %collective-permute-start = (bf16[32,16,64]{2,1,0:T(8,128)(2,1)S(1)}, bf16[32,16,64]{2,1,0:T(8,128)(2,1)S(1)}, u32[]{:S(2)}, u32[]{:S(2)}) collective-permute-start(bf16[32,16,64]{2,1,0:T(8,128)(2,1)S(1)} %copy-done.27), channel_id=1, source_target_pairs={{0,16},{16,32},{32,48},{48,64},{64,80},{80,96},{96,112},{112,0},{1... | collective-permute-start | bytes 196616 | tf_op jit(solution)/shard_map/ppermute | solution.py:20
  30.4 74.3 %collective-permute-start.4 = (bf16[32,16,64]{2,1,0:T(8,128)(2,1)S(1)}, bf16[32,16,64]{2,1,0:T(8,128)(2,1)S(1)}, u32[]{:S(2)}, u32[]{:S(2)}) collective-permute-start(bf16[32,16,64]{2,1,0:T(8,128)(2,1)S(1)} %copy-done.27), channel_id=1, source_target_pairs={{0,112},{16,0},{32,16},{48,32},{64,48},{80,64},{96,80},{112,96},{1... | collective-permute-start | bytes 196616 | tf_op jit(solution)/shard_map/ppermute | solution.py:22
  104.6 4.4 %collective-permute-start.1 = (bf16[32,16,64]{2,1,0:T(8,128)(2,1)S(1)}, bf16[32,16,64]{2,1,0:T(8,128)(2,1)S(1)}, u32[]{:S(2)}, u32[]{:S(2)}) collective-permute-start(bf16[32,16,64]{2,1,0:T(8,128)(2,1)S(1)} %collective-permute-done), channel_id=1, source_target_pairs={{0,16},{16,32},{32,48},{48,64},{64,80},{80,96},{96,112},{112,0},{1... | collective-permute-start | bytes 196616 | tf_op jit(solution)/shard_map/ppermute | solution.py:20
  104.6 4.4 %collective-permute-start.5 = (bf16[32,16,64]{2,1,0:T(8,128)(2,1)S(1)}, bf16[32,16,64]{2,1,0:T(8,128)(2,1)S(1)}, u32[]{:S(2)}, u32[]{:S(2)}) collective-permute-start(bf16[32,16,64]{2,1,0:T(8,128)(2,1)S(1)} %collective-permute-done.4), channel_id=1, source_target_pairs={{0,112},{16,0},{32,16},{48,32},{64,48},{80,64},{96,80},{112,96},{1... | collective-permute-start | bytes 196616 | tf_op jit(solution)/shard_map/ppermute | solution.py:22
  109.0 4.4 %copy-start.28 = (bf16[32,16,64]{2,1,0:T(8,128)(2,1)}, bf16[32,16,64]{2,1,0:T(8,128)(2,1)S(1)}, u32[]{:S(2)}) copy-start(bf16[32,16,64]{2,1,0:T(8,128)(2,1)S(1)} %collective-permute-done.1) | copy-start | bytes 196612
  109.0 4.4 %collective-permute-start.2 = (bf16[32,16,64]{2,1,0:T(8,128)(2,1)S(1)}, bf16[32,16,64]{2,1,0:T(8,128)(2,1)S(1)}, u32[]{:S(2)}, u32[]{:S(2)}) collective-permute-start(bf16[32,16,64]{2,1,0:T(8,128)(2,1)S(1)} %collective-permute-done.1), channel_id=1, source_target_pairs={{0,16},{16,32},{32,48},{48,64},{64,80},{80,96},{96,112},{112,0},{1... | collective-permute-start | bytes 196616 | tf_op jit(solution)/shard_map/ppermute | solution.py:20
  109.0 4.4 %copy-start.29 = (bf16[32,16,64]{2,1,0:T(8,128)(2,1)}, bf16[32,16,64]{2,1,0:T(8,128)(2,1)S(1)}, u32[]{:S(2)}) copy-start(bf16[32,16,64]{2,1,0:T(8,128)(2,1)S(1)} %collective-permute-done.5) | copy-start | bytes 196612
  109.1 4.4 %collective-permute-start.6 = (bf16[32,16,64]{2,1,0:T(8,128)(2,1)S(1)}, bf16[32,16,64]{2,1,0:T(8,128)(2,1)S(1)}, u32[]{:S(2)}, u32[]{:S(2)}) collective-permute-start(bf16[32,16,64]{2,1,0:T(8,128)(2,1)S(1)} %collective-permute-done.5), channel_id=1, source_target_pairs={{0,112},{16,0},{32,16},{48,32},{64,48},{80,64},{96,80},{112,96},{1... | collective-permute-start | bytes 196616 | tf_op jit(solution)/shard_map/ppermute | solution.py:22
  113.4 4.5 %collective-permute-start.3 = (bf16[32,16,64]{2,1,0:T(8,128)(2,1)S(1)}, bf16[32,16,64]{2,1,0:T(8,128)(2,1)}, u32[]{:S(2)}, u32[]{:S(2)}) collective-permute-start(bf16[32,16,64]{2,1,0:T(8,128)(2,1)S(1)} %collective-permute-done.2), channel_id=1, source_target_pairs={{0,16},{16,32},{32,48},{48,64},{64,80},{80,96},{96,112},{112,0},{1... | collective-permute-start | bytes 196616 | tf_op jit(solution)/shard_map/ppermute | solution.py:20
  133.1 23.0 %all-to-all-start.1 = ((bf16[16,64,512]{2,1,0:T(8,128)(2,1)}), bf16[16,64,512]{2,1,0:T(8,128)(2,1)S(1)}, u32[]{:S(2)}, u32[]{:S(2)}) async-start(bf16[16,64,512]{2,1,0:T(8,128)(2,1)} %convolution_convert_fusion.1), calls=%async_computation.1 | async-start | bytes 2097152 | tf_op jit(solution)/shard_map/all_to_all | solution.py:172
  145.3 16.8 %copy-start.40 = (s32[16]{0:T(128)S(1)}, s32[16]{0:T(128)}, u32[]{:S(2)}) copy-start(s32[16]{0:T(128)} %copy-done.39) | copy-start | bytes 196
  157.1 65.8 %all-to-all-start.2 = ((bf16[16,64,2048]{2,1,0:T(8,128)(2,1)}), bf16[16,64,2048]{2,1,0:T(8,128)(2,1)}, u32[]{:S(2)}, u32[]{:S(2)}) async-start(bf16[16,64,2048]{2,1,0:T(8,128)(2,1)} %convolution_convert_fusion), calls=%async_computation.2 | async-start | bytes 8388608 | tf_op jit(solution)/shard_map/all_to_all | solution.py:171
  277.8 4.5 %copy-start.24 = (f32[4,128,192]{1,2,0:T(8,128)S(1)}, f32[4,128,192]{1,2,0:T(8,128)}, u32[]{:S(2)}) copy-start(f32[4,128,192]{1,2,0:T(8,128)} %get-tuple-element.45) | copy-start | bytes 1179652
  278.1 5.3 %copy-start.23 = (f32[4,128,192]{1,2,0:T(8,128)S(1)}, f32[4,128,192]{1,2,0:T(8,128)}, u32[]{:S(2)}) copy-start(f32[4,128,192]{1,2,0:T(8,128)} %get-tuple-element.47) | copy-start | bytes 1179652
  279.1 5.4 %copy-start.22 = (f32[4,128,192]{1,2,0:T(8,128)S(1)}, f32[4,128,192]{1,2,0:T(8,128)}, u32[]{:S(2)}) copy-start(f32[4,128,192]{1,2,0:T(8,128)} %get-tuple-element.49) | copy-start | bytes 1179652
  285.6 4.5 %copy-start.16 = (f32[4,128,192]{1,2,0:T(8,128)S(1)}, f32[4,128,192]{1,2,0:T(8,128)}, u32[]{:S(2)}) copy-start(f32[4,128,192]{1,2,0:T(8,128)} %get-tuple-element.61) | copy-start | bytes 1179652
  285.9 5.3 %copy-start.15 = (f32[4,128,192]{1,2,0:T(8,128)S(1)}, f32[4,128,192]{1,2,0:T(8,128)}, u32[]{:S(2)}) copy-start(f32[4,128,192]{1,2,0:T(8,128)} %get-tuple-element.63) | copy-start | bytes 1179652
  286.9 5.4 %copy-start.14 = (f32[4,128,192]{1,2,0:T(8,128)S(1)}, f32[4,128,192]{1,2,0:T(8,128)}, u32[]{:S(2)}) copy-start(f32[4,128,192]{1,2,0:T(8,128)} %get-tuple-element.65) | copy-start | bytes 1179652
  (33 other events, 71.0 us)
Sparse Core Ops, SparseCore 0:
  9.0 38.3 all-gather.3
  49.1 27.6 all-gather.5
